TPU v7x, 256 devices: a whole 4x4x8 slice. The times are simulated.
256 devices in a mesh: prow: 16 (over z, core), pcol: 16 (over y, x).
Axes of the slice: x: 4, y: 4, z: 8, core: 2. Of those that a mesh axis runs over, the one named last changes fastest.
Arguments:
- kernel: float32 [3, 16, 256, 3, 16, 256], P(None, 'prow', None, None, 'pcol'), as said below
Outputs:
- factored: float32 [3, 16, 256, 3, 16, 256], P(None, 'prow', None, None, 'pcol')
Inputs may be any that keep to these rules, and one draw needn't show every extreme that they name: kernel is symmetric (entry (a, b) equals entry (b, a)); every diagonal entry is 1.1, every off-diagonal entry lies in (0, 1], and the matrix is positive definite with smallest eigenvalue at least 0.1.
All inputs are finite; a program needn't handle non-finite values.
Results may differ from a plain program's by a relative error of at most 0.0003.
Values sent between devices are 32-bit elements; how exact they have to be, the bound alone decides.
No kernel may reach another device: no remote copies, remote signals or barrier semaphores. Data moves between devices by JAX's collectives and lax.ppermute only.
A program may use at most 64 MiB of HBM per device.

v0:
```python
import jax
import jax.numpy as jnp
from jax import lax
from jax.sharding import PartitionSpec as P

HIGH = lax.Precision.HIGHEST


def chol_and_inverse(block, eye):
    lower = jnp.linalg.cholesky(block)
    inverse = jax.scipy.linalg.solve_triangular(lower, eye, lower=True)
    return lower, inverse


def on_device(kernel):
    prow = lax.axis_index("prow")
    pcol = lax.axis_index("pcol")
    rows = lax.axis_size("prow")
    cols = lax.axis_size("pcol")
    lbr, blk, lbc = kernel.shape[0], kernel.shape[2], kernel.shape[3]
    work = kernel.reshape(lbr, blk, lbc, blk)
    eye = jnp.eye(blk, dtype=jnp.float32)
    zero = jnp.zeros((blk, blk), jnp.float32)

    corner_blk = work[0, :, 0, :]
    slots = jnp.stack(
        [
            jnp.where((prow == 0) & (pcol == 0), corner_blk, zero),
            jnp.where((prow == 1) & (pcol == 0), corner_blk, zero),
            jnp.where((prow == 1) & (pcol == 1), corner_blk, zero),
        ]
    )
    corner = lax.psum(slots, ("prow", "pcol"))

    own_col = work[:, :, 0, :]
    row_slots = jnp.stack(
        [jnp.where(pcol == 0, own_col, 0.0), jnp.where(pcol == 1, own_col, 0.0)]
    )
    row_panel = lax.psum(row_slots, "pcol")

    own_row = work[0]
    col_slots = jnp.stack(
        [jnp.where(prow == 0, own_row, 0.0), jnp.where(prow == 1, own_row, 0.0)]
    )
    col_panel = lax.psum(col_slots, "prow")

    l0, w0 = chol_and_inverse(corner[0], eye)
    p10 = jnp.dot(corner[1], w0.T, precision=HIGH)
    s11 = corner[2] - jnp.dot(p10, p10.T, precision=HIGH)
    l1, w1 = chol_and_inverse(s11, eye)

    r0 = jnp.einsum("aik,jk->aij", row_panel[0], w0, precision=HIGH)
    r1 = row_panel[1] - jnp.einsum("aik,jk->aij", r0, p10, precision=HIGH)
    r1 = jnp.einsum("aik,jk->aij", r1, w1, precision=HIGH)

    c0t = jnp.einsum("ik,kbj->bij", w0, col_panel[0], precision=HIGH)
    c1t = jnp.transpose(col_panel[1], (1, 0, 2)) - jnp.einsum(
        "ik,bkj->bij", p10, c0t, precision=HIGH
    )
    c1t = jnp.einsum("ik,bkj->bij", w1, c1t, precision=HIGH)

    left = jnp.concatenate([r0, r1], axis=2)
    right = jnp.concatenate([c0t, c1t], axis=1)
    trailing = work - jnp.einsum("aik,bkj->aibj", left, right, precision=HIGH)

    row_ids = jnp.arange(lbr, dtype=jnp.int32) * rows + prow
    col_ids = jnp.arange(lbc, dtype=jnp.int32) * cols + pcol
    ri = row_ids[:, None, None, None]
    cj = col_ids[None, None, :, None]
    rk = row_ids[:, None, None]
    col0 = jnp.where(rk == 0, l0[None], r0)[:, :, None, :]
    col1 = jnp.where(rk == 0, 0.0, jnp.where(rk == 1, l1[None], r1))[:, :, None, :]
    out = jnp.where(cj == 0, col0, jnp.where(cj == 1, col1, trailing))
    out = jnp.where((ri < 2) & (cj > ri), 0.0, out)
    return out.reshape(kernel.shape)


def solution(mesh):
    spec = P(None, "prow", None, None, "pcol", None)
    return jax.shard_map(
        on_device, mesh=mesh, in_specs=(spec,), out_specs=spec, check_vma=False
    )
```

profile of v0, /device:TPU:2, one launch (start us, length us, event | category | flops | bytes accessed | tf_op | source)
XLA Modules:
  0.0 512.3 jit_solution(17465115443136146933)
XLA Ops:
  6.5 5.5 %copy.2 = f32[3,1,256,3,1,256]{2,5,3,0,4,1:T(8,128)S(1)} copy(f32[3,1,256,3,1,256]{5,4,3,2,1,0:T(1,128)} %param.4) | data formatting | bytes 4718592 | tf_op args[0]
  13.1 1.1 slice-done
  14.3 1.3 pad_maximum_fusion.1
  15.8 1.2 pad_maximum_fusion
  17.7 252.8 %all-reduce.5.cloned.1.call-done = f32[3,256,256]{1,2,0:T(8,128)} async-done(((f32[3,256,256]{1,2,0:T(8,128)}), f32[3,256,256]{1,2,0:T(8,128)}) %all-reduce.5.cloned.1.call-update) | async-done | bytes 786448 | tf_op jit(solution)/shard_map/psum | solution.py:33
  272.7 11.7 %cholesky.130 = f32[128,128]{1,0:T(8,128)S(1)} custom-call(f32[128,128]{1,0:T(8,128)S(1)} %cholesky.194), custom_call_target="Cholesky" | custom-call | tf_op jit(solution)/shard_map/jit(cholesky)/cholesky | solution.py:10
  284.4 9.8 %custom-call.13 = f32[1,128,128]{1,2,0:T(8,128)S(1)} custom-call(f32[1,128,128]{2,1,0:T(8,128)S(1)} %get-tuple-element.59), custom_call_target="InvertDiagBlocksLowerTriangular" | custom-call | tf_op jit(solution)/shard_map/jit(cholesky)/cholesky | solution.py:10
  294.7 11.7 %cholesky.147 = f32[128,128]{1,0:T(8,128)S(1)} custom-call(f32[128,128]{1,0:T(8,128)S(1)} %convolution_subtract_fusion.5), custom_call_target="Cholesky" | custom-call | tf_op jit(solution)/shard_map/jit(cholesky)/cholesky | solution.py:10
  309.3 3.9 while.4
  310.0 1.3 bitcast_dynamic-update-slice_fusion.4
  312.0 1.3 bitcast_dynamic-update-slice_fusion.4
  313.3 20.0 %custom-call.14 = f32[2,128,128]{1,2,0:T(8,128)S(1)} custom-call(f32[2,128,128]{2,1,0:T(8,128)S(1)} %get-tuple-element.21), custom_call_target="InvertDiagBlocksLowerTriangular" | custom-call | tf_op jit(solution)/shard_map/jit(_solve_triangular)/triangular_solve | solution.py:11
  334.9 1.5 fusion.8
  336.5 1.4 convolution_subtract_fusion.1
  338.7 11.7 %cholesky.164 = f32[128,128]{1,0:T(8,128)S(1)} custom-call(f32[128,128]{1,0:T(8,128)S(1)} %cholesky.197), custom_call_target="Cholesky" | custom-call | tf_op jit(solution)/shard_map/jit(cholesky)/cholesky | solution.py:10
  350.5 9.8 %custom-call.15 = f32[1,128,128]{1,2,0:T(8,128)S(1)} custom-call(f32[1,128,128]{2,1,0:T(8,128)S(1)} %get-tuple-element.55), custom_call_target="InvertDiagBlocksLowerTriangular" | custom-call | tf_op jit(solution)/shard_map/jit(cholesky)/cholesky | solution.py:10
  361.4 1.1 convolution_subtract_fusion.4
  362.5 11.7 %cholesky.181 = f32[128,128]{1,0:T(8,128)S(1)} custom-call(f32[128,128]{1,0:T(8,128)S(1)} %convolution_subtract_fusion.4), custom_call_target="Cholesky" | custom-call | tf_op jit(solution)/shard_map/jit(cholesky)/cholesky | solution.py:10
  376.8 1.7 fusion.15
  378.6 3.9 while.5
  379.4 1.2 bitcast_dynamic-update-slice_fusion.5
  381.2 1.2 bitcast_dynamic-update-slice_fusion.5
  382.4 19.7 %custom-call.16 = f32[2,128,128]{1,2,0:T(8,128)S(1)} custom-call(f32[2,128,128]{2,1,0:T(8,128)S(1)} %get-tuple-element.22), custom_call_target="InvertDiagBlocksLowerTriangular" | custom-call | tf_op jit(solution)/shard_map/jit(_solve_triangular)/triangular_solve | solution.py:11
  402.1 1.8 copy.10
  404.0 1.8 copy.4
  406.4 1.8 fusion.24
  408.2 2.1 convolution_bitcast_fusion.2
  411.3 1.7 convolution_bitcast_fusion
  413.1 75.3 %all-reduce.7.cloned.1.call-done = f32[2,3,256,256]{2,3,1,0:T(8,128)} async-done(((f32[2,3,256,256]{2,3,1,0:T(8,128)}), f32[2,3,256,256]{2,3,1,0:T(8,128)}) %all-reduce.7.cloned.1.call-update) | async-done | bytes 1572880 | tf_op jit(solution)/shard_map/psum | solution.py:39
  488.3 2.1 fusion.5
  492.8 6.2 %select_bitcast_fusion = f32[3,1,256,3,1,256]{2,5,3,0,4,1:T(8,128)} fusion(f32[3,256,256]{1,2,0:T(8,128)S(1)} %get-tuple-element.66, f32[3,256,256]{1,2,0:T(8,128)S(1)} %fusion.5, f32[3,256,256]{2,1,0:T(8,128)S(1)} %copy-done, f32[3,256,256]{2,1,0:T(8,128)S(1)} %convolution_bitcast_fusion.2, f32[3,256,256]{1,2,0:T(8,128)S(1)} %get-tuple-element.61, ...), kind=kOutput, calls=%fused_computation.4 | convolution fusion | flops 3627024384 | bytes 9437199 | tf_op jit(solution)/shard_map/aik,bkj->aibj/dot_general | solution.py:64
  499.0 6.6 %copy.15 = f32[3,1,256,3,1,256]{5,4,3,2,1,0:T(1,128)} copy(f32[3,1,256,3,1,256]{2,5,3,0,4,1:T(8,128)} %select_bitcast_fusion) | data formatting | bytes 4718592 | tf_op jit(solution)/shard_map/reshape | solution.py:75
  (93 shorter events, 17.4 us)
Async XLA Ops:
  6.5 264.0 %all-reduce.5.cloned.1.call-start = ((), (), s32[]{:S(2)}) async-start(), calls=%async_computation | async-start | bytes 1572864 | tf_op jit(solution)/shard_map/psum | solution.py:33
  13.0 1.1 slice-start
  13.1 395.1 %all-reduce.9.cloned.1.call-start = ((), (), s32[]{:S(2)}) async-start(), calls=%async_computation.2 | async-start | bytes 3145728 | tf_op jit(solution)/shard_map/psum | solution.py:45
  15.6 472.7 %all-reduce.7.cloned.1.call-start = ((), (), s32[]{:S(2)}) async-start(), calls=%async_computation.1 | async-start | bytes 3145728 | tf_op jit(solution)/shard_map/psum | solution.py:39
  313.3 20.0 %copy-start.15 = (s32[2,2]{1,0:T(2,128)}, s32[2,2]{1,0:T(2,128)S(1)}, u32[]{:S(2)}) copy-start(s32[2,2]{1,0:T(2,128)S(1)} %get-tuple-element.177) | copy-start | bytes 52
  334.2 0.7 copy-start.1
  338.0 0.7 copy-start.12
  338.7 39.8 %copy-start.16 = (s32[2,2]{1,0:T(2,128)S(1)}, s32[2,2]{1,0:T(2,128)}, u32[]{:S(2)}) copy-start(s32[2,2]{1,0:T(2,128)} %copy-done.15) | copy-start | bytes 52
  374.2 2.6 copy-start.11
  402.1 3.7 copy-start.13
  406.1 2.1 copy-start.2
  408.2 2.1 copy-start.5
  410.3 0.9 copy-start.3
  410.4 1.0 copy-start.7
  488.3 2.1 copy-start.6
  490.5 0.9 copy-start.4
  490.5 1.0 copy-start.8
  490.5 1.1 copy-start.9
  490.5 1.1 copy-start.10
  490.5 1.1 copy-start.14
  491.6 1.1 copy-start
Sparse Core Ops, SparseCore 0:
  13.2 257.3 all-reduce.4
  273.0 113.0 all-reduce.8
  389.4 98.8 all-reduce.6
where the time goes:
time: 523 us; the launch traced here: 512 us
  waiting for transfers between devices  328 us (63%)
  other arithmetic  116 us (22%)
  local copies, waits for them, and re-layouts  27.6 us (5%)
  matrix products  23.6 us (5%)
  between operations  16.3 us (3%)
    psum x1, waiting for transfers between devices, on_device(): corner = lax.psum(slots, ('prow', 'pcol'))  253 us
    psum x1, waiting for transfers between devices, on_device(): row_panel = lax.psum(row_slots, 'pcol')  75.3 us
    another operation x13, other arithmetic, chol_and_inverse(): lower = jnp.linalg.cholesky(block)  68.7 us
    another operation x5, other arithmetic, chol_and_inverse(): inverse = jax.scipy.linalg.solve_triangular(lower, eye, lower=True)  42.2 us
  transfers between devices with their start and end apart: 3, of which 2 were waited for; matrix products, arithmetic and copies ran while one was open for 28% of the time, Pallas kernels for 0%

commit v1 on v0

v1 whole, which is shorter than its diff:
```python
import jax
import jax.numpy as jnp
from jax import lax
from jax.sharding import PartitionSpec as P

HIGH = lax.Precision.HIGHEST


def chol_and_inverse(block, eye):
    lower = jnp.linalg.cholesky(block)
    inverse = jax.scipy.linalg.solve_triangular(lower, eye, lower=True)
    return lower, inverse


def from_two_sources(own, axis, sources):
    peers = lax.axis_size(axis)
    shape = own.shape
    flat = own.reshape(-1, shape[-1])
    spare = -flat.shape[0] % peers
    flat = jnp.pad(flat, [(0, spare), (0, 0)])
    pieces = flat.reshape(peers, -1, shape[-1])
    mine = lax.all_to_all(pieces, axis, 0, 0, tiled=False)
    kept = jnp.stack([mine[s] for s in sources])
    spread = lax.all_to_all(
        jnp.broadcast_to(kept[None], (peers, *kept.shape)), axis, 0, 0, tiled=False
    )
    whole = jnp.swapaxes(spread, 0, 1).reshape(len(sources), -1, shape[-1])
    whole = whole[:, : flat.shape[0] - spare]
    return whole.reshape(len(sources), *shape)


def on_device(kernel):
    prow = lax.axis_index("prow")
    pcol = lax.axis_index("pcol")
    rows = lax.axis_size("prow")
    cols = lax.axis_size("pcol")
    lbr, blk, lbc = kernel.shape[0], kernel.shape[2], kernel.shape[3]
    work = kernel.reshape(lbr, blk, lbc, blk)
    eye = jnp.eye(blk, dtype=jnp.float32)

    ytop = from_two_sources(work[0], "prow", (0, 1))
    y0c = ytop[0][:, 0, :]
    y1c = ytop[1][:, 0, :]
    extra = jnp.where(pcol == 0, jnp.stack([y0c, y1c]), jnp.stack([y1c, jnp.zeros_like(y1c)]))
    own = jnp.concatenate([work[:, :, 0, :], extra], axis=0)
    xs = from_two_sources(own, "pcol", (0, 1))
    x0 = xs[0][:lbr]
    x1 = xs[1][:lbr]
    m00 = xs[0][lbr]
    m10 = xs[0][lbr + 1]
    m11 = xs[1][lbr]

    l0, w0 = chol_and_inverse(m00, eye)
    p10 = jnp.dot(m10, w0.T, precision=HIGH)
    s11 = m11 - jnp.dot(p10, p10.T, precision=HIGH)
    l1, w1 = chol_and_inverse(s11, eye)

    r0 = jnp.einsum("aik,jk->aij", x0, w0, precision=HIGH)
    r1 = x1 - jnp.einsum("aik,jk->aij", r0, p10, precision=HIGH)
    r1 = jnp.einsum("aik,jk->aij", r1, w1, precision=HIGH)

    c0t = jnp.einsum("ik,kbj->bij", w0, ytop[0], precision=HIGH)
    c1t = jnp.transpose(ytop[1], (1, 0, 2)) - jnp.einsum(
        "ik,bkj->bij", p10, c0t, precision=HIGH
    )
    c1t = jnp.einsum("ik,bkj->bij", w1, c1t, precision=HIGH)

    left = jnp.concatenate([r0, r1], axis=2)
    right = jnp.concatenate([c0t, c1t], axis=1)
    trailing = work - jnp.einsum("aik,bkj->aibj", left, right, precision=HIGH)

    row_ids = jnp.arange(lbr, dtype=jnp.int32) * rows + prow
    col_ids = jnp.arange(lbc, dtype=jnp.int32) * cols + pcol
    ri = row_ids[:, None, None, None]
    cj = col_ids[None, None, :, None]
    rk = row_ids[:, None, None]
    col0 = jnp.where(rk == 0, l0[None], r0)[:, :, None, :]
    col1 = jnp.where(rk == 0, 0.0, jnp.where(rk == 1, l1[None], r1))[:, :, None, :]
    out = jnp.where(cj == 0, col0, jnp.where(cj == 1, col1, trailing))
    out = jnp.where((ri < 2) & (cj > ri), 0.0, out)
    return out.reshape(kernel.shape)


def solution(mesh):
    spec = P(None, "prow", None, None, "pcol", None)
    return jax.shard_map(
        on_device, mesh=mesh, in_specs=(spec,), out_specs=spec, check_vma=False
    )
```

time: 523 us -> 359 us (0.69)
  the two profiles are of different devices: /device:TPU:2 before, /device:TPU:1 now
where the time goes in v1:
time: 359 us; the launch traced here: 353 us
  other arithmetic  122 us (34%)
  waiting for transfers between devices  69.4 us (19%)
  local copies, waits for them, and re-layouts  59.3 us (17%)
  blocking collectives  59.1 us (16%)
  matrix products  31.5 us (9%)
  starting transfers between devices  9.06 us (3%)
    another operation x14, other arithmetic, chol_and_inverse(): lower = jnp.linalg.cholesky(block)  73 us
    all_to_all x2, waiting for transfers between devices, from_two_sources(): lax.all_to_all(jnp.broadcast_to(kept[None], (peers, *kept.shape)), axis,...  69.4 us
    all_to_all x2, blocking collectives, from_two_sources(): mine = lax.all_to_all(pieces, axis, 0, 0, tiled=False)  59.1 us
    another operation x5, other arithmetic, chol_and_inverse(): inverse = jax.scipy.linalg.solve_triangular(lower, eye, lower=True)  45.3 us
    another operation x15, local copies, waits for them, and re-layouts, chol_and_inverse(): inverse = jax.scipy.linalg.solve_triangular(lower, eye, lower=True)  15.1 us
    all_to_all x2, starting transfers between devices, from_two_sources(): lax.all_to_all(jnp.broadcast_to(kept[None], (peers, *kept.shape)), axis,...  9.06 us
  transfers between devices with their start and end apart: 2, of which 2 were waited for; matrix products, arithmetic and copies ran while one was open for 2% of the time, Pallas kernels for 0%

profile of v1, /device:TPU:1, one launch (start us, length us, event | category | flops | bytes accessed | tf_op | source)
XLA Modules:
  0.0 353.3 jit_solution(13451875521586901230)
XLA Ops:
  0.0 3.4 slice_reduce_fusion
  3.8 32.7 %all_to_all.20 = f32[16,48,256]{2,1,0:T(8,128)S(1)} all-to-all(f32[16,48,256]{2,1,0:T(8,128)S(1)} %reshape.132), channel_id=1, replica_groups=mesh['prow'=16,'pcol'=16] {'prow'}, dimensions={0} | all-to-all | bytes 1572864 | tf_op jit(solution)/shard_map/all_to_all | solution.py:22
  37.9 4.4 %all-to-all-start.1 = ((f32[16,2,48,256]{3,2,1,0:T(8,128)}), f32[16,2,48,256]{3,2,1,0:T(8,128)}, u32[]{:S(2)}, u32[]{:S(2)}) async-start(f32[16,2,48,256]{3,2,1,0:T(8,128)} %broadcast_in_dim.98), calls=%async_computation.1 | async-start | bytes 3145728 | tf_op jit(solution)/shard_map/all_to_all | solution.py:24
  44.0 2.1 slice_bitcast_fusion
  46.0 34.2 %all-to-all-done.1 = f32[16,2,48,256]{3,2,1,0:T(8,128)} async-done(((f32[16,2,48,256]{3,2,1,0:T(8,128)}), f32[16,2,48,256]{3,2,1,0:T(8,128)}, u32[]{:S(2)}, u32[]{:S(2)}) %all-to-all-start.1) | async-done | bytes 1572896 | tf_op jit(solution)/shard_map/all_to_all | solution.py:24
  80.2 2.6 fusion.42
  88.2 26.4 %all_to_all.21 = f32[16,80,256]{2,1,0:T(8,128)S(1)} all-to-all(f32[16,80,256]{2,1,0:T(8,128)S(1)} %bitcast.146), channel_id=1, replica_groups=mesh['prow'=16,'pcol'=16] {'pcol'}, dimensions={0} | all-to-all | bytes 2621440 | tf_op jit(solution)/shard_map/all_to_all | solution.py:22
  116.5 4.6 %all-to-all-start.3 = ((f32[16,2,80,256]{3,2,1,0:T(8,128)}), f32[16,2,80,256]{3,2,1,0:T(8,128)}, u32[]{:S(2)}, u32[]{:S(2)}) async-start(f32[16,2,80,256]{3,2,1,0:T(8,128)} %broadcast_in_dim.99), calls=%async_computation.3 | async-start | bytes 5242880 | tf_op jit(solution)/shard_map/all_to_all | solution.py:24
  124.2 35.2 %all-to-all-done.3 = f32[16,2,80,256]{3,2,1,0:T(8,128)} async-done(((f32[16,2,80,256]{3,2,1,0:T(8,128)}), f32[16,2,80,256]{3,2,1,0:T(8,128)}, u32[]{:S(2)}, u32[]{:S(2)}) %all-to-all-start.3) | async-done | bytes 2621472 | tf_op jit(solution)/shard_map/all_to_all | solution.py:24
  159.4 1.9 copy.66
  164.9 11.7 %cholesky.130 = f32[128,128]{1,0:T(8,128)S(1)} custom-call(f32[128,128]{1,0:T(8,128)S(1)} %cholesky.194), custom_call_target="Cholesky" | custom-call | tf_op jit(solution)/shard_map/jit(cholesky)/cholesky | solution.py:10
  177.2 9.8 %custom-call.13 = f32[1,128,128]{1,2,0:T(8,128)S(1)} custom-call(f32[1,128,128]{2,1,0:T(8,128)S(1)} %get-tuple-element.58), custom_call_target="InvertDiagBlocksLowerTriangular" | custom-call | tf_op jit(solution)/shard_map/jit(cholesky)/cholesky | solution.py:10
  188.3 11.7 %cholesky.147 = f32[128,128]{1,0:T(8,128)S(1)} custom-call(f32[128,128]{1,0:T(8,128)S(1)} %convolution_subtract_fusion.5), custom_call_target="Cholesky" | custom-call | tf_op jit(solution)/shard_map/jit(cholesky)/cholesky | solution.py:10
  207.0 7.0 %while.4 = (s32[]{:T(128)}, f32[256,256]{1,0:T(8,128)}, s32[2,2]{1,0:T(2,128)}, f32[2,128,128]{2,1,0:T(8,128)S(1)}, s32[]{:T(128)}) while((s32[]{:T(128)}, f32[256,256]{1,0:T(8,128)}, s32[2,2]{1,0:T(2,128)}, f32[2,128,128]{2,1,0:T(8,128)S(1)}, s32[]{:T(128)}) %tuple.52), condition=%wide.while_cond, body=%wide.while_body.sunk | while | flops 2 | bytes 131181 | solution.py:11
  208.3 2.2 bitcast_dynamic-update-slice_fusion.4
  211.8 2.1 bitcast_dynamic-update-slice_fusion.4
  214.6 20.9 %custom-call.14 = f32[2,128,128]{1,2,0:T(8,128)S(1)} custom-call(f32[2,128,128]{2,1,0:T(8,128)} %copy-done.12), custom_call_target="InvertDiagBlocksLowerTriangular" | custom-call | tf_op jit(solution)/shard_map/jit(_solve_triangular)/triangular_solve | solution.py:11
  243.8 2.1 convolution_subtract_fusion.1
  249.4 11.7 %cholesky.164 = f32[128,128]{1,0:T(8,128)S(1)} custom-call(f32[128,128]{1,0:T(8,128)S(1)} %cholesky.197), custom_call_target="Cholesky" | custom-call | tf_op jit(solution)/shard_map/jit(cholesky)/cholesky | solution.py:10
  262.4 9.8 %custom-call.15 = f32[1,128,128]{1,2,0:T(8,128)S(1)} custom-call(f32[1,128,128]{2,1,0:T(8,128)S(1)} %get-tuple-element.54), custom_call_target="InvertDiagBlocksLowerTriangular" | custom-call | tf_op jit(solution)/shard_map/jit(cholesky)/cholesky | solution.py:10
  275.0 11.9 %cholesky.181 = f32[128,128]{1,0:T(8,128)S(1)} custom-call(f32[128,128]{1,0:T(8,128)S(1)} %convolution_subtract_fusion.4), custom_call_target="Cholesky" | custom-call | tf_op jit(solution)/shard_map/jit(cholesky)/cholesky | solution.py:10
  292.4 7.0 %while.5 = (s32[]{:T(128)}, f32[256,256]{1,0:T(8,128)}, s32[2,2]{1,0:T(2,128)}, f32[2,128,128]{2,1,0:T(8,128)S(1)}, s32[]{:T(128)}) while((s32[]{:T(128)}, f32[256,256]{1,0:T(8,128)}, s32[2,2]{1,0:T(2,128)}, f32[2,128,128]{2,1,0:T(8,128)S(1)}, s32[]{:T(128)}) %tuple.58), condition=%wide.while_cond.clone, body=%wide.while_body.clone.sunk | while | flops 2 | bytes 131181 | solution.py:11
  293.7 2.2 bitcast_dynamic-update-slice_fusion.5
  297.2 2.1 bitcast_dynamic-update-slice_fusion.5
  299.3 20.3 %custom-call.16 = f32[2,128,128]{1,2,0:T(8,128)} custom-call(f32[2,128,128]{2,1,0:T(8,128)S(1)} %get-tuple-element.22), custom_call_target="InvertDiagBlocksLowerTriangular" | custom-call | tf_op jit(solution)/shard_map/jit(_solve_triangular)/triangular_solve | solution.py:11
  323.9 3.4 convolution_subtract_fusion
  330.9 2.8 fusion.4
  335.5 2.3 broadcast_select_fusion
  337.8 2.3 copy.36
  340.1 2.3 copy.42
  342.4 6.9 %select_bitcast_fusion = f32[3,1,256,3,1,256]{5,2,3,0,4,1:T(8,128)S(1)} fusion(f32[3,256,256]{1,2,0:T(8,128)} %get-tuple-element.65, f32[3,256,256]{1,2,0:T(8,128)S(1)} %fusion.11, f32[3,256,256]{2,1,0:T(8,128)} %convolution_bitcast_fusion, f32[3,256,256]{2,1,0:T(8,128)} %convolution_bitcast_fusion.2, f32[3,256,256]{2,1,0:T(8,128)} %copy.42, ...), kind=kOutput, calls=%fused_computation.6 | convolution fusion | flops 3627024384 | bytes 9437199 | tf_op jit(solution)/shard_map/aik,bkj->aibj/dot_general | solution.py:70
  349.3 3.8 %copy.48 = f32[3,1,256,3,1,256]{5,4,3,2,1,0:T(1,128)} copy(f32[3,1,256,3,1,256]{5,2,3,0,4,1:T(8,128)S(1)} %select_bitcast_fusion) | data formatting | bytes 4718592 | tf_op jit(solution)/shard_map/reshape | solution.py:81
  (98 shorter events, 60.3 us)
Async XLA Ops:
  37.9 4.5 %copy-start = (f32[3,1,256,3,1,256]{5,4,3,2,1,0:T(1,128)S(1)}, f32[3,1,256,3,1,256]{5,4,3,2,1,0:T(1,128)}, u32[]{:S(2)}) copy-start(f32[3,1,256,3,1,256]{5,4,3,2,1,0:T(1,128)} %param.4) | copy-start | bytes 7077892
  37.9 42.3 %all-to-all-start.1 = ((f32[16,2,48,256]{3,2,1,0:T(8,128)}), f32[16,2,48,256]{3,2,1,0:T(8,128)}, u32[]{:S(2)}, u32[]{:S(2)}) async-start(f32[16,2,48,256]{3,2,1,0:T(8,128)} %broadcast_in_dim.98), calls=%async_computation.1 | async-start | bytes 3145728 | tf_op jit(solution)/shard_map/all_to_all | solution.py:24
  86.8 1.3 copy-start.5
  116.5 43.0 %all-to-all-start.3 = ((f32[16,2,80,256]{3,2,1,0:T(8,128)}), f32[16,2,80,256]{3,2,1,0:T(8,128)}, u32[]{:S(2)}, u32[]{:S(2)}) async-start(f32[16,2,80,256]{3,2,1,0:T(8,128)} %broadcast_in_dim.99), calls=%async_computation.3 | async-start | bytes 5242880 | tf_op jit(solution)/shard_map/all_to_all | solution.py:24
  162.6 1.1 copy-start.1
  164.9 70.6 %copy-start.6 = (f32[256,256]{1,0:T(8,128)S(1)}, f32[256,256]{1,0:T(8,128)}, u32[]{:S(2)}) copy-start(f32[256,256]{1,0:T(8,128)} %fusion.15) | copy-start | bytes 786436
  187.3 0.7 copy-start.10
  188.2 49.1 %copy-start.3 = (f32[256,3,256]{2,0,1:T(8,128)S(1)}, f32[256,3,256]{2,0,1:T(8,128)}, u32[]{:S(2)}) copy-start(f32[256,3,256]{2,0,1:T(8,128)} %copy.30) | copy-start | bytes 2359300
  213.9 0.7 copy-start.12
  235.5 3.6 %copy-start.2 = (f32[1,16,80,256]{3,2,1,0:T(8,128)S(1)}, f32[1,16,80,256]{3,2,1,0:T(8,128)}, u32[]{:S(2)}) copy-start(f32[1,16,80,256]{3,2,1,0:T(8,128)} %copy-done.1) | copy-start | bytes 3932164
  248.7 0.7 copy-start.11
  330.9 2.8 copy-start.7
  333.7 1.8 copy-start.4
  333.7 1.8 copy-start.8
  333.7 1.8 copy-start.9
  333.8 1.8 copy-start.13

commit v2 on v1

--- a/solution.py
+++ b/solution.py
@@ -7,8 +7,17 @@
 
 
 def chol_and_inverse(block, eye):
-    lower = jnp.linalg.cholesky(block)
-    inverse = jax.scipy.linalg.solve_triangular(lower, eye, lower=True)
+    h = block.shape[0] // 2
+    small = eye[:h, :h]
+    la = jnp.linalg.cholesky(block[:h, :h])
+    wa = jax.scipy.linalg.solve_triangular(la, small, lower=True)
+    lb = jnp.dot(block[h:, :h], wa.T, precision=HIGH)
+    lc = jnp.linalg.cholesky(block[h:, h:] - jnp.dot(lb, lb.T, precision=HIGH))
+    wc = jax.scipy.linalg.solve_triangular(lc, small, lower=True)
+    wb = -jnp.dot(wc, jnp.dot(lb, wa, precision=HIGH), precision=HIGH)
+    zero = jnp.zeros_like(small)
+    lower = jnp.block([[la, zero], [lb, lc]])
+    inverse = jnp.block([[wa, zero], [wb, wc]])
     return lower, inverse
 
 

time: 359 us -> 329 us (0.916)
  other arithmetic: 122 us -> 104 us
  local copies, waits for them, and re-layouts: 59.3 us -> 45.9 us
    another operation x19 -> x20, other arithmetic: 118 us -> 97.8 us  [the longest x6 25.6 us: chol_and_inverse(): lc = jnp.linalg.cholesky(block[h:, h:] - jnp.dot(lb, lb.T, precision=HIGH))]
    another operation x19 -> x2, local copies, waits for them, and re-layouts: 15.9 us -> 0.82 us  [chol_and_inverse(): wc = jax.scipy.linalg.solve_triangular(lc, small, lower=True)]
    dot_general x0 -> x8, matrix products: none -> 7.6 us  [the longest x2 2.89 us: chol_and_inverse(): lc = jnp.linalg.cholesky(block[h:, h:] - jnp.dot(lb, lb.T, precision=HIGH))]
    another operation x10 -> x4, matrix products: 9.31 us -> 3.61 us  [the longest x2 2.24 us: chol_and_inverse(): wa = jax.scipy.linalg.solve_triangular(la, small, lower=True)]
    concatenate x0 -> x2, local copies, waits for them, and re-layouts: none -> 3.6 us  [chol_and_inverse(): lower = jnp.block([[la, zero], [lb, lc]])]
where the time goes in v2:
time: 329 us; the launch traced here: 323 us
  other arithmetic  104 us (32%)
  waiting for transfers between devices  70.1 us (21%)
  blocking collectives  59.1 us (18%)
  local copies, waits for them, and re-layouts  45.9 us (14%)
  matrix products  33.3 us (10%)
  starting transfers between devices  9.35 us (3%)
    all_to_all x2, waiting for transfers between devices, from_two_sources(): lax.all_to_all(jnp.broadcast_to(kept[None], (peers, *kept.shape)), axis,...  70.1 us
    all_to_all x2, blocking collectives, from_two_sources(): mine = lax.all_to_all(pieces, axis, 0, 0, tiled=False)  59.1 us
    another operation x6, other arithmetic, chol_and_inverse(): lc = jnp.linalg.cholesky(block[h:, h:] - jnp.dot(lb, lb.T, precision=HIGH))  25.6 us
    another operation x6, other arithmetic, chol_and_inverse(): la = jnp.linalg.cholesky(block[:h, :h])  24.9 us
    another operation x4, other arithmetic, chol_and_inverse(): wc = jax.scipy.linalg.solve_triangular(lc, small, lower=True)  23.7 us
    another operation x4, other arithmetic, chol_and_inverse(): wa = jax.scipy.linalg.solve_triangular(la, small, lower=True)  23.5 us
    all_to_all x2, starting transfers between devices, from_two_sources(): lax.all_to_all(jnp.broadcast_to(kept[None], (peers, *kept.shape)), axis,...  9.35 us
    dot_general x1, matrix products, on_device(): trailing = work - jnp.einsum('aik,bkj->aibj', left, right, precision=HIGH)  7.15 us
  transfers between devices with their start and end apart: 2, of which 2 were waited for; matrix products, arithmetic and copies ran while one was open for 2% of the time, Pallas kernels for 0%

profile of v2, /device:TPU:1, one launch (start us, length us, event | category | flops | bytes accessed | tf_op | source)
XLA Modules:
  0.0 322.8 jit_solution(12030417150146159587)
XLA Ops:
  0.0 3.4 %slice_reduce_fusion = f32[256,3,256]{2,1,0:T(4,128)S(1)} fusion(f32[3,1,256,3,1,256]{5,4,3,2,1,0:T(1,128)} %param.4), kind=kLoop, calls=%fused_computation.22 | loop fusion | bytes 1572864 | tf_op jit(solution)/shard_map/slice | solution.py:50
  3.8 32.7 %all_to_all.20 = f32[16,48,256]{2,1,0:T(8,128)S(1)} all-to-all(f32[16,48,256]{2,1,0:T(8,128)S(1)} %reshape.125), channel_id=1, replica_groups=mesh['prow'=16,'pcol'=16] {'prow'}, dimensions={0} | all-to-all | bytes 1572864 | tf_op jit(solution)/shard_map/all_to_all | solution.py:31
  37.9 4.4 %all-to-all-start.1 = ((f32[16,2,48,256]{3,2,1,0:T(8,128)}), f32[16,2,48,256]{3,2,1,0:T(8,128)}, u32[]{:S(2)}, u32[]{:S(2)}) async-start(f32[16,2,48,256]{3,2,1,0:T(8,128)} %broadcast_in_dim.98), calls=%async_computation.1 | async-start | bytes 3145728 | tf_op jit(solution)/shard_map/all_to_all | solution.py:33
  44.0 2.1 slice_bitcast_fusion
  46.0 34.2 %all-to-all-done.1 = f32[16,2,48,256]{3,2,1,0:T(8,128)} async-done(((f32[16,2,48,256]{3,2,1,0:T(8,128)}), f32[16,2,48,256]{3,2,1,0:T(8,128)}, u32[]{:S(2)}, u32[]{:S(2)}) %all-to-all-start.1) | async-done | bytes 1572896 | tf_op jit(solution)/shard_map/all_to_all | solution.py:33
  80.2 2.6 fusion.64
  88.2 26.4 %all_to_all.21 = f32[16,80,256]{2,1,0:T(8,128)S(1)} all-to-all(f32[16,80,256]{2,1,0:T(8,128)S(1)} %bitcast.130), channel_id=1, replica_groups=mesh['prow'=16,'pcol'=16] {'pcol'}, dimensions={0} | all-to-all | bytes 2621440 | tf_op jit(solution)/shard_map/all_to_all | solution.py:31
  114.7 1.8 broadcast_in_dim.99
  116.5 4.9 %all-to-all-start.3 = ((f32[16,2,80,256]{3,2,1,0:T(8,128)}), f32[16,2,80,256]{3,2,1,0:T(8,128)}, u32[]{:S(2)}, u32[]{:S(2)}) async-start(f32[16,2,80,256]{3,2,1,0:T(8,128)} %broadcast_in_dim.99), calls=%async_computation.3 | async-start | bytes 5242880 | tf_op jit(solution)/shard_map/all_to_all | solution.py:33
  123.3 35.9 %all-to-all-done.3 = f32[16,2,80,256]{3,2,1,0:T(8,128)} async-done(((f32[16,2,80,256]{3,2,1,0:T(8,128)}), f32[16,2,80,256]{3,2,1,0:T(8,128)}, u32[]{:S(2)}, u32[]{:S(2)}) %all-to-all-start.3) | async-done | bytes 2621472 | tf_op jit(solution)/shard_map/all_to_all | solution.py:33
  159.2 1.9 copy.99
  165.5 11.7 %cholesky.74 = f32[128,128]{1,0:T(8,128)S(1)} custom-call(f32[128,128]{1,0:T(8,128)S(1)} %fusion.40), custom_call_target="Cholesky" | custom-call | tf_op jit(solution)/shard_map/jit(cholesky)/cholesky | solution.py:12
  179.2 10.4 %custom-call.8 = f32[1,128,128]{1,2,0:T(8,128)} custom-call(f32[1,128,128]{2,1,0:T(8,128)S(1)} %get-tuple-element.13), custom_call_target="InvertDiagBlocksLowerTriangular" | custom-call | tf_op jit(solution)/shard_map/jit(_solve_triangular)/triangular_solve | solution.py:13
  194.1 11.7 %cholesky.85 = f32[128,128]{1,0:T(8,128)S(1)} custom-call(f32[128,128]{1,0:T(8,128)S(1)} %fusion.38), custom_call_target="Cholesky" | custom-call | tf_op jit(solution)/shard_map/jit(cholesky)/cholesky | solution.py:15
  207.8 9.9 %custom-call.9 = f32[1,128,128]{1,2,0:T(8,128)S(1)} custom-call(f32[1,128,128]{2,1,0:T(8,128)S(1)} %get-tuple-element.11), custom_call_target="InvertDiagBlocksLowerTriangular" | custom-call | tf_op jit(solution)/shard_map/jit(_solve_triangular)/triangular_solve | solution.py:16
  218.5 1.7 convolution_bitcast_fusion.2
  223.1 1.8 copy.93
  227.9 11.7 %cholesky.96 = f32[128,128]{1,0:T(8,128)S(1)} custom-call(f32[128,128]{1,0:T(8,128)S(1)} %fusion.36), custom_call_target="Cholesky" | custom-call | tf_op jit(solution)/shard_map/jit(cholesky)/cholesky | solution.py:12
  241.8 10.4 %custom-call.10 = f32[1,128,128]{1,2,0:T(8,128)} custom-call(f32[1,128,128]{2,1,0:T(8,128)S(1)} %get-tuple-element.9), custom_call_target="InvertDiagBlocksLowerTriangular" | custom-call | tf_op jit(solution)/shard_map/jit(_solve_triangular)/triangular_solve | solution.py:13
  254.4 1.8 convolution_subtract_fusion.2
  259.4 1.8 copy.58
  261.2 3.6 %convolution_subtract_fusion = f32[3,256,256]{2,1,0:T(8,128)} fusion(f32[3,256,256]{1,2,0:T(8,128)S(1)} %fusion.12, f32[5,256,256]{2,1,0:T(8,128)} %bitcast.132, f32[256,256]{1,0:T(8,128)S(1)} %fusion.6), kind=kOutput, calls=%fused_computation.14 | convolution fusion | flops 604176384 | bytes 2621440 | tf_op jit(solution)/shard_map/aik,jk->aij/dot_general | solution.py:68
  267.1 12.5 %cholesky.107 = f32[128,128]{1,0:T(8,128)S(1)} custom-call(f32[128,128]{1,0:T(8,128)} %fusion.34), custom_call_target="Cholesky" | custom-call | tf_op jit(solution)/shard_map/jit(cholesky)/cholesky | solution.py:15
  281.5 11.3 %custom-call.11 = f32[1,128,128]{1,2,0:T(8,128)} custom-call(f32[1,128,128]{2,1,0:T(8,128)} %get-tuple-element.6), custom_call_target="InvertDiagBlocksLowerTriangular" | custom-call | tf_op jit(solution)/shard_map/jit(_solve_triangular)/triangular_solve | solution.py:16
  298.0 1.8 copy.68
  299.8 2.9 fusion.4
  302.7 1.8 convolution_bitcast_fusion
  304.5 2.3 broadcast_select_fusion
  306.8 2.3 copy.61
  309.1 2.3 copy.72
  311.4 7.2 %select_bitcast_fusion = f32[3,1,256,3,1,256]{5,2,3,0,4,1:T(8,128)S(1)} fusion(f32[3,256,256]{1,2,0:T(8,128)} %get-tuple-element.21, f32[3,256,256]{1,2,0:T(8,128)S(1)} %fusion.12, f32[3,256,256]{2,1,0:T(8,128)} %convolution_bitcast_fusion, f32[3,256,256]{2,1,0:T(8,128)} %convolution_bitcast_fusion.2, f32[3,256,256]{2,1,0:T(8,128)} %copy.72, ...), kind=kOutput, calls=%fused_computation.2 | convolution fusion | flops 3627024384 | bytes 9437199 | tf_op jit(solution)/shard_map/aik,bkj->aibj/dot_general | solution.py:79
  318.5 3.8 %copy.78 = f32[3,1,256,3,1,256]{5,4,3,2,1,0:T(1,128)} copy(f32[3,1,256,3,1,256]{5,2,3,0,4,1:T(8,128)S(1)} %select_bitcast_fusion) | data formatting | bytes 4718592 | tf_op jit(solution)/shard_map/reshape | solution.py:90
  (92 shorter events, 46.7 us)
Async XLA Ops:
  37.9 4.4 %copy-start = (f32[3,1,256,3,1,256]{5,4,3,2,1,0:T(1,128)S(1)}, f32[3,1,256,3,1,256]{5,4,3,2,1,0:T(1,128)}, u32[]{:S(2)}) copy-start(f32[3,1,256,3,1,256]{5,4,3,2,1,0:T(1,128)} %param.4) | copy-start | bytes 7077892
  37.9 42.3 %all-to-all-start.1 = ((f32[16,2,48,256]{3,2,1,0:T(8,128)}), f32[16,2,48,256]{3,2,1,0:T(8,128)}, u32[]{:S(2)}, u32[]{:S(2)}) async-start(f32[16,2,48,256]{3,2,1,0:T(8,128)} %broadcast_in_dim.98), calls=%async_computation.1 | async-start | bytes 3145728 | tf_op jit(solution)/shard_map/all_to_all | solution.py:33
  86.8 1.3 copy-start.5
  116.5 42.7 %all-to-all-start.3 = ((f32[16,2,80,256]{3,2,1,0:T(8,128)}), f32[16,2,80,256]{3,2,1,0:T(8,128)}, u32[]{:S(2)}, u32[]{:S(2)}) async-start(f32[16,2,80,256]{3,2,1,0:T(8,128)} %broadcast_in_dim.99), calls=%async_computation.3 | async-start | bytes 5242880 | tf_op jit(solution)/shard_map/all_to_all | solution.py:33
  162.4 1.1 copy-start.1
  164.2 54.3 %copy-start.3 = (f32[256,3,256]{2,0,1:T(8,128)S(1)}, f32[256,3,256]{2,0,1:T(8,128)}, u32[]{:S(2)}) copy-start(f32[256,3,256]{2,0,1:T(8,128)} %copy.50) | copy-start | bytes 2359300
  165.3 24.3 %copy-start.8 = (f32[1,256,256]{1,2,0:T(8,128)}, f32[1,256,256]{1,2,0:T(8,128)S(1)}, u32[]{:S(2)}) copy-start(f32[1,256,256]{1,2,0:T(8,128)S(1)} %copy.92) | copy-start | bytes 786436
  218.1 2.1 copy-start.2
  226.3 0.7 copy-start.9
  259.4 5.5 %copy-start.12 = (f32[128,128]{0,1:T(8,128)S(1)}, f32[128,128]{0,1:T(8,128)}, u32[]{:S(2)}) copy-start(f32[128,128]{0,1:T(8,128)} %convolution_subtract_fusion.2) | copy-start | bytes 196612
  293.9 0.6 copy-start.11
  299.8 2.9 copy-start.10
  299.8 4.7 %copy-start.4 = (f32[3,256,256]{2,1,0:T(8,128)S(1)}, f32[3,256,256]{2,1,0:T(8,128)}, u32[]{:S(2)}) copy-start(f32[3,256,256]{2,1,0:T(8,128)} %convolution_subtract_fusion) | copy-start | bytes 2359300
  299.8 4.7 %copy-start.6 = (f32[256,256]{0,1:T(8,128)S(1)}, f32[256,256]{0,1:T(8,128)}, u32[]{:S(2)}) copy-start(f32[256,256]{0,1:T(8,128)} %copy.58) | copy-start | bytes 786436
  299.8 4.7 %copy-start.7 = (f32[256,256]{0,1:T(8,128)S(1)}, f32[256,256]{0,1:T(8,128)}, u32[]{:S(2)}) copy-start(f32[256,256]{0,1:T(8,128)} %copy.68) | copy-start | bytes 786436
  299.8 4.7 %copy-start.13 = (pred[3]{0:T(512)(128)(4,1)S(1)}, pred[3]{0:T(512)(128)(4,1)}, u32[]{:S(2)}) copy-start(pred[3]{0:T(512)(128)(4,1)} %get-tuple-element.27) | copy-start | bytes 13

commit v3 on v2

--- a/solution.py
+++ b/solution.py
@@ -9,10 +9,12 @@
 def chol_and_inverse(block, eye):
     h = block.shape[0] // 2
     small = eye[:h, :h]
-    la = jnp.linalg.cholesky(block[:h, :h])
+    la = jnp.linalg.cholesky(block[:h, :h], symmetrize_input=False)
     wa = jax.scipy.linalg.solve_triangular(la, small, lower=True)
     lb = jnp.dot(block[h:, :h], wa.T, precision=HIGH)
-    lc = jnp.linalg.cholesky(block[h:, h:] - jnp.dot(lb, lb.T, precision=HIGH))
+    lc = jnp.linalg.cholesky(
+        block[h:, h:] - jnp.dot(lb, lb.T, precision=HIGH), symmetrize_input=False
+    )
     wc = jax.scipy.linalg.solve_triangular(lc, small, lower=True)
     wb = -jnp.dot(wc, jnp.dot(lb, wa, precision=HIGH), precision=HIGH)
     zero = jnp.zeros_like(small)
@@ -80,13 +82,13 @@
 
     row_ids = jnp.arange(lbr, dtype=jnp.int32) * rows + prow
     col_ids = jnp.arange(lbc, dtype=jnp.int32) * cols + pcol
-    ri = row_ids[:, None, None, None]
-    cj = col_ids[None, None, :, None]
     rk = row_ids[:, None, None]
-    col0 = jnp.where(rk == 0, l0[None], r0)[:, :, None, :]
-    col1 = jnp.where(rk == 0, 0.0, jnp.where(rk == 1, l1[None], r1))[:, :, None, :]
-    out = jnp.where(cj == 0, col0, jnp.where(cj == 1, col1, trailing))
-    out = jnp.where((ri < 2) & (cj > ri), 0.0, out)
+    col0 = jnp.where(rk == 0, l0[None], r0)
+    col1 = jnp.where(rk == 0, 0.0, jnp.where(rk == 1, l1[None], r1))
+    first_col = jnp.where(pcol == 0, col0, jnp.where(pcol == 1, col1, trailing[:, :, 0, :]))
+    out = trailing.at[:, :, 0, :].set(first_col)
+    upper = (prow < 2) & (col_ids > prow)
+    out = out.at[0].set(jnp.where(upper[None, :, None], 0.0, out[0]))
     return out.reshape(kernel.shape)
 
 

time: 329 us -> 317 us (0.964)
  matrix products: 33.3 us -> 26.9 us
  local copies, waits for them, and re-layouts: 45.9 us -> 42.6 us
    select_n x2 -> x0, local copies, waits for them, and re-layouts: 4.56 us -> none  [the longest x1 2.28 us: on_device(): jnp.where(rk == 0, 0.0, jnp.where(rk == 1, l1[None], r1))[:, :, None, :]]
    scatter x0 -> x1, local copies, waits for them, and re-layouts: none -> 4.29 us  [on_device(): out = out.at[0].set(jnp.where(upper[None, :, None], 0.0, out[0]))]
    reshape x1 -> x0, local copies, waits for them, and re-layouts: 3.83 us -> none  [on_device(): return out.reshape(kernel.shape)]
    unnamed x31 -> x35, local copies, waits for them, and re-layouts: 6.98 us -> 9.01 us
where the time goes in v3:
time: 317 us; the launch traced here: 311 us
  other arithmetic  103 us (32%)
  waiting for transfers between devices  69.5 us (22%)
  blocking collectives  59.3 us (19%)
  local copies, waits for them, and re-layouts  42.6 us (13%)
  matrix products  26.9 us (8%)
  starting transfers between devices  8.93 us (3%)
    all_to_all x2, waiting for transfers between devices, from_two_sources(): lax.all_to_all(jnp.broadcast_to(kept[None], (peers, *kept.shape)), axis,...  69.5 us
    all_to_all x2, blocking collectives, from_two_sources(): mine = lax.all_to_all(pieces, axis, 0, 0, tiled=False)  59.3 us
    another operation x6, other arithmetic, chol_and_inverse(): jnp.linalg.cholesky(block[h:, h:] - jnp.dot(lb, lb.T, precision=HIGH), sy...  26.1 us
    another operation x6, other arithmetic, chol_and_inverse(): la = jnp.linalg.cholesky(block[:h, :h], symmetrize_input=False)  24.9 us
    another operation x4, other arithmetic, chol_and_inverse(): wc = jax.scipy.linalg.solve_triangular(lc, small, lower=True)  24.7 us
    another operation x4, other arithmetic, chol_and_inverse(): wa = jax.scipy.linalg.solve_triangular(la, small, lower=True)  22.1 us
    unnamed x35, local copies, waits for them, and re-layouts  9.01 us
    all_to_all x2, starting transfers between devices, from_two_sources(): lax.all_to_all(jnp.broadcast_to(kept[None], (peers, *kept.shape)), axis,...  8.93 us
  transfers between devices with their start and end apart: 2, of which 2 were waited for; matrix products, arithmetic and copies ran while one was open for 2% of the time, Pallas kernels for 0%

profile of v3, /device:TPU:1, one launch (start us, length us, event | category | flops | bytes accessed | tf_op | source)
XLA Modules:
  0.0 310.9 jit_solution(5158471315864353169)
XLA Ops:
  0.0 3.4 %slice_reduce_fusion = f32[256,3,256]{2,1,0:T(4,128)S(1)} fusion(f32[3,1,256,3,1,256]{5,4,3,2,1,0:T(1,128)} %param.8), kind=kLoop, calls=%fused_computation.29 | loop fusion | bytes 1572864 | tf_op jit(solution)/shard_map/slice | solution.py:52
  3.8 32.7 %all_to_all.20 = f32[16,48,256]{2,1,0:T(8,128)S(1)} all-to-all(f32[16,48,256]{2,1,0:T(8,128)S(1)} %reshape.137), channel_id=1, replica_groups=mesh['prow'=16,'pcol'=16] {'prow'}, dimensions={0} | all-to-all | bytes 1572864 | tf_op jit(solution)/shard_map/all_to_all | solution.py:33
  37.9 4.3 %all-to-all-start.1 = ((f32[16,2,48,256]{3,2,1,0:T(8,128)}), f32[16,2,48,256]{3,2,1,0:T(8,128)}, u32[]{:S(2)}, u32[]{:S(2)}) async-start(f32[16,2,48,256]{3,2,1,0:T(8,128)} %broadcast_in_dim.65), calls=%async_computation.1 | async-start | bytes 3145728 | tf_op jit(solution)/shard_map/all_to_all | solution.py:35
  42.2 5.5 %copy.33 = f32[3,1,256,3,1,256]{2,5,0,3,4,1:T(8,128)S(1)} copy(f32[3,1,256,3,1,256]{5,4,3,2,1,0:T(1,128)} %param.8) | data formatting | bytes 4718592 | tf_op args[0]
  48.6 31.4 %all-to-all-done.1 = f32[16,2,48,256]{3,2,1,0:T(8,128)} async-done(((f32[16,2,48,256]{3,2,1,0:T(8,128)}), f32[16,2,48,256]{3,2,1,0:T(8,128)}, u32[]{:S(2)}, u32[]{:S(2)}) %all-to-all-start.1) | async-done | bytes 1572896 | tf_op jit(solution)/shard_map/all_to_all | solution.py:35
  80.1 2.4 fusion.69
  83.8 1.5 copy.35
  86.0 2.4 squeeze.36
  93.1 2.8 copy.36
  95.9 26.6 %all_to_all.21 = f32[16,80,256]{2,1,0:T(8,128)S(1)} all-to-all(f32[16,80,256]{2,1,0:T(8,128)} %bitcast.134), channel_id=1, replica_groups=mesh['prow'=16,'pcol'=16] {'pcol'}, dimensions={0} | all-to-all | bytes 2621440 | tf_op jit(solution)/shard_map/all_to_all | solution.py:33
  122.6 1.8 broadcast_in_dim.66
  124.4 4.6 %all-to-all-start.3 = ((f32[16,2,80,256]{3,2,1,0:T(8,128)}), f32[16,2,80,256]{3,2,1,0:T(8,128)}, u32[]{:S(2)}, u32[]{:S(2)}) async-start(f32[16,2,80,256]{3,2,1,0:T(8,128)} %broadcast_in_dim.66), calls=%async_computation.3 | async-start | bytes 5242880 | tf_op jit(solution)/shard_map/all_to_all | solution.py:35
  129.1 38.0 %all-to-all-done.3 = f32[16,2,80,256]{3,2,1,0:T(8,128)} async-done(((f32[16,2,80,256]{3,2,1,0:T(8,128)}), f32[16,2,80,256]{3,2,1,0:T(8,128)}, u32[]{:S(2)}, u32[]{:S(2)}) %all-to-all-start.3) | async-done | bytes 2621472 | tf_op jit(solution)/shard_map/all_to_all | solution.py:35
  167.1 3.0 fusion.68
  171.2 11.7 %cholesky.75 = f32[128,128]{1,0:T(8,128)S(1)} custom-call(f32[128,128]{1,0:T(8,128)S(1)} %slice.186), custom_call_target="Cholesky" | custom-call | tf_op jit(solution)/shard_map/jit(cholesky)/cholesky | solution.py:12
  184.9 9.8 %custom-call.8 = f32[1,128,128]{1,2,0:T(8,128)S(1)} custom-call(f32[1,128,128]{2,1,0:T(8,128)S(1)} %get-tuple-element.37), custom_call_target="InvertDiagBlocksLowerTriangular" | custom-call | tf_op jit(solution)/shard_map/jit(_solve_triangular)/triangular_solve | solution.py:13
  196.5 11.7 %cholesky.86 = f32[128,128]{1,0:T(8,128)S(1)} custom-call(f32[128,128]{1,0:T(8,128)S(1)} %convolution_subtract_fusion.4), custom_call_target="Cholesky" | custom-call | tf_op jit(solution)/shard_map/jit(cholesky)/cholesky | solution.py:15
  210.2 10.0 %custom-call.9 = f32[1,128,128]{1,2,0:T(8,128)S(1)} custom-call(f32[1,128,128]{2,1,0:T(8,128)S(1)} %get-tuple-element.35), custom_call_target="InvertDiagBlocksLowerTriangular" | custom-call | tf_op jit(solution)/shard_map/jit(_solve_triangular)/triangular_solve | solution.py:18
  223.7 11.7 %cholesky.97 = f32[128,128]{1,0:T(8,128)S(1)} custom-call(f32[128,128]{1,0:T(8,128)S(1)} %slice.193), custom_call_target="Cholesky" | custom-call | tf_op jit(solution)/shard_map/jit(cholesky)/cholesky | solution.py:12
  237.4 9.8 %custom-call.10 = f32[1,128,128]{1,2,0:T(8,128)S(1)} custom-call(f32[1,128,128]{2,1,0:T(8,128)S(1)} %get-tuple-element.33), custom_call_target="InvertDiagBlocksLowerTriangular" | custom-call | tf_op jit(solution)/shard_map/jit(_solve_triangular)/triangular_solve | solution.py:13
  249.4 3.2 %convolution_bitcast_fusion.2 = f32[3,256,256]{2,1,0:T(8,128)} fusion(f32[256,3,256]{2,1,0:T(4,128)} %squeeze.36, f32[128,128]{1,0:T(8,128)S(1)} %fusion.29, f32[128,128]{1,0:T(8,128)S(1)} %copy.38, f32[128,128]{1,0:T(8,128)S(1)} %convolution_negate_fusion.1), kind=kOutput, calls=%fused_computation.10 | convolution fusion | flops 604241920 | bytes 1769472 | tf_op jit(solution)/shard_map/ik,kbj->bij/dot_general | solution.py:73
  253.5 1.7 fusion.18
  256.0 1.8 copy.49
  257.8 12.9 %cholesky.108 = f32[128,128]{1,0:T(8,128)S(1)} custom-call(f32[128,128]{1,0:T(8,128)} %convolution_subtract_fusion.3), custom_call_target="Cholesky" | custom-call | tf_op jit(solution)/shard_map/jit(cholesky)/cholesky | solution.py:15
  272.1 2.2 select_bitcast_fusion
  274.2 1.6 select_maximum_fusion
  275.8 1.8 copy.51
  277.6 3.7 %fusion.4 = f32[3,256,256]{1,2,0:T(8,128)} fusion(f32[3,256,256]{2,1,0:T(8,128)} %convolution_bitcast_fusion.2, f32[256,3,256]{0,2,1:T(8,128)} %copy-done.3, f32[256,256]{1,0:T(8,128)S(1)} %fusion.14), kind=kOutput, calls=%fused_computation.11 | convolution fusion | flops 604176384 | bytes 2621440 | tf_op jit(solution)/shard_map/ik,bkj->bij/dot_general | solution.py:74
  281.2 11.3 %custom-call.11 = f32[1,128,128]{1,2,0:T(8,128)} custom-call(f32[1,128,128]{2,1,0:T(8,128)} %get-tuple-element.31), custom_call_target="InvertDiagBlocksLowerTriangular" | custom-call | tf_op jit(solution)/shard_map/jit(_solve_triangular)/triangular_solve | solution.py:18
  296.2 2.5 convolution_subtract_fusion.1
  300.6 4.9 %convolution_subtract_fusion = f32[3,256,3,256]{1,3,0,2:T(8,128)S(1)} fusion(f32[3,256,256]{1,2,0:T(8,128)S(1)} %fusion.21, f32[3,256,256]{1,2,0:T(8,128)S(1)} %fusion.18, f32[3,256,256]{2,1,0:T(8,128)S(1)} %convolution_bitcast_fusion, f32[3,256,256]{2,1,0:T(8,128)S(1)} %copy-done, f32[3,1,256,3,1,256]{2,5,0,3,4,1:T(8,128)S(1)} %copy.33), kind=kOutput, calls=%fused_computation | convolution fusion | flops 3625254912 | bytes 7864320 | tf_op jit(solution)/shard_map/aik,bkj->aibj/dot_general | solution.py:81
  306.4 4.3 %copy.53 = f32[3,1,256,3,1,256]{5,4,3,2,1,0:T(1,128)} copy(f32[3,1,256,3,1,256]{2,5,0,3,4,1:T(8,128)S(1)} %fusion.7) | data formatting | bytes 4718592 | tf_op jit(solution)/shard_map/scatter | solution.py:91
  (83 shorter events, 33.2 us)
Async XLA Ops:
  37.9 42.2 %all-to-all-start.1 = ((f32[16,2,48,256]{3,2,1,0:T(8,128)}), f32[16,2,48,256]{3,2,1,0:T(8,128)}, u32[]{:S(2)}, u32[]{:S(2)}) async-start(f32[16,2,48,256]{3,2,1,0:T(8,128)} %broadcast_in_dim.65), calls=%async_computation.1 | async-start | bytes 3145728 | tf_op jit(solution)/shard_map/all_to_all | solution.py:35
  85.3 5.4 %copy-start.3 = (f32[256,3,256]{0,2,1:T(8,128)}, f32[256,3,256]{0,2,1:T(8,128)S(1)}, u32[]{:S(2)}) copy-start(f32[256,3,256]{0,2,1:T(8,128)S(1)} %copy.35) | copy-start | bytes 2359300
  90.6 1.4 copy-start.5
  124.4 42.7 %all-to-all-start.3 = ((f32[16,2,80,256]{3,2,1,0:T(8,128)}), f32[16,2,80,256]{3,2,1,0:T(8,128)}, u32[]{:S(2)}, u32[]{:S(2)}) async-start(f32[16,2,80,256]{3,2,1,0:T(8,128)} %broadcast_in_dim.66), calls=%async_computation.3 | async-start | bytes 5242880 | tf_op jit(solution)/shard_map/all_to_all | solution.py:35
  170.1 1.1 copy-start.1
  220.6 32.0 %copy-start.7 = (f32[128,128]{1,0:T(8,128)}, f32[128,128]{1,0:T(8,128)S(1)}, u32[]{:S(2)}) copy-start(f32[128,128]{1,0:T(8,128)S(1)} %copy.38) | copy-start | bytes 196612
  220.9 31.7 %copy-start.6 = (f32[128,128]{1,0:T(8,128)}, f32[128,128]{1,0:T(8,128)S(1)}, u32[]{:S(2)}) copy-start(f32[128,128]{1,0:T(8,128)S(1)} %convolution_negate_fusion.1) | copy-start | bytes 196612
  249.4 4.1 %copy-start.2 = (f32[1,16,80,256]{3,2,0,1:T(8,128)S(1)}, f32[1,16,80,256]{3,2,0,1:T(8,128)}, u32[]{:S(2)}) copy-start(f32[1,16,80,256]{3,2,0,1:T(8,128)} %copy-done.1) | copy-start | bytes 3932164
  249.4 5.8 %copy-start.12 = (f32[128,128]{1,0:T(8,128)S(1)}, f32[128,128]{1,0:T(8,128)}, u32[]{:S(2)}) copy-start(f32[128,128]{1,0:T(8,128)} %get-tuple-element.38) | copy-start | bytes 196612
  249.4 5.8 %copy-start.13 = (f32[128,128]{1,0:T(8,128)S(1)}, f32[128,128]{1,0:T(8,128)}, u32[]{:S(2)}) copy-start(f32[128,128]{1,0:T(8,128)} %get-tuple-element.36) | copy-start | bytes 196612
  249.4 5.8 %copy-start.14 = (f32[128,128]{1,0:T(8,128)S(1)}, f32[128,128]{1,0:T(8,128)}, u32[]{:S(2)}) copy-start(f32[128,128]{1,0:T(8,128)} %copy.48) | copy-start | bytes 196612
  270.7 0.6 copy-start.15
  293.6 0.6 copy-start.11
  295.0 3.8 %copy-start.4 = (f32[3,256,256]{1,2,0:T(8,128)S(1)}, f32[3,256,256]{1,2,0:T(8,128)}, u32[]{:S(2)}) copy-start(f32[3,256,256]{1,2,0:T(8,128)} %fusion.4) | copy-start | bytes 2359300
  295.0 3.8 %copy-start.10 = (f32[128,128]{1,0:T(8,128)S(1)}, f32[128,128]{1,0:T(8,128)}, u32[]{:S(2)}) copy-start(f32[128,128]{1,0:T(8,128)} %copy.41) | copy-start | bytes 196612
  298.8 1.8 copy-start
  300.5 5.0 %copy-start.8 = (f32[256,256]{0,1:T(8,128)S(1)}, f32[256,256]{0,1:T(8,128)}, u32[]{:S(2)}) copy-start(f32[256,256]{0,1:T(8,128)} %copy.49) | copy-start | bytes 786436
  300.6 5.0 %copy-start.9 = (f32[256,256]{0,1:T(8,128)S(1)}, f32[256,256]{0,1:T(8,128)}, u32[]{:S(2)}) copy-start(f32[256,256]{0,1:T(8,128)} %copy.51) | copy-start | bytes 786436
